TPU v7x, 256 devices: a whole 4x4x8 slice. The times are simulated.
256 devices in a mesh: wide: 32 (over z_hi, y, core), narrow: 8 (over z_lo, x).
Axes of the slice: x: 4, y: 4, z: 8 (z_hi: 4, z_lo: 2; z = z_hi * 2 + z_lo), core: 2. Of those that a mesh axis runs over, the one named last changes fastest.
Arguments:
- residual: bfloat16 [256, 8192], P('wide'), may hold values from -60 to 60
- norm_gain: float32 [8192], replicated, may hold values from 0.1 to 1.9
- w_query: bfloat16 [8192, 8192], P('wide', 'narrow'), may hold values from -0.0625 to 0.0625
- key_projection_weight: bfloat16 [8192, 1024], P('wide', 'narrow'), may hold values from -0.0625 to 0.0625
- value_projection_weight: bfloat16 [8192, 1024], P('wide', 'narrow'), may hold values from -0.0625 to 0.0625
- w_out: bfloat16 [8192, 8192], P('narrow', 'wide'), may hold values from -0.5 to 0.5
- cache_keys: bfloat16 [256, 8, 1024, 128], P('wide', 'narrow'), may hold values from -480 to 480
- stored_values: bfloat16 [256, 8, 1024, 128], P('wide', 'narrow'), may hold values from -24 to 24
- lengths: int32 [256], P('wide'), may hold values from 1 to 1024, as said below
- w_enc: bfloat16 [8192, 65536], P('narrow', 'wide'), may hold values from -0.0625 to 0.0625
- b_enc: float32 [65536], P('wide'), may hold values from -3 to 3
- w_dec: bfloat16 [65536, 8192], P('wide', 'narrow'), may hold values from -0.0625 to 0.0625
- b_dec: float32 [8192], P('narrow'), may hold values from -3 to 3
- clamp_index: int32 [256, 8], replicated, may hold values from 0 to 65535, as said below
- clamp_value: float32 [256, 8], replicated, may hold values from 10 to 40
Outputs:
- steered: bfloat16 [256, 8192], P('wide', 'narrow')
Inputs may be any that keep to these rules, and one draw needn't show every extreme that they name: `lengths`: row 0 has all 1024 slots filled. `clamp_index`: the 8 latents of a row are distinct.
All inputs are finite; a program needn't handle non-finite values.
Results may differ from a plain program's by a relative error of at most 0.014.
The roundings to bfloat16 on the way count: a program that leaves them out, or rounds other values in their place, can miss the bound.
Values may be sent and summed in bfloat16 or wider, within the bound.
No kernel may reach another device: no remote copies, remote signals or barrier semaphores. Data moves between devices by JAX's collectives and lax.ppermute only.
A program may use at most 64 MiB of HBM per device.

v0:
```python
import math
import jax
import jax.numpy as jnp
from jax import lax
from jax.sharding import PartitionSpec as P

HEAD_WIDTH = 128
rope_base = 500000.0


def rotary(vectors, positions):
    halfway = vectors.shape[-1] // 2
    counter = jnp.arange(halfway, dtype=jnp.float32)
    inverse = rope_base ** (-2.0 * counter / vectors.shape[-1])
    angles = positions.astype(jnp.float32)[:, None] * inverse[None, :]
    cosine = jnp.cos(angles)[:, None, :]
    sine = jnp.sin(angles)[:, None, :]
    first_half = vectors[..., :halfway]
    second_half = vectors[..., halfway:]
    return jnp.concatenate(
        [first_half * cosine - second_half * sine, second_half * cosine + first_half * sine],
        axis=-1,
    )


def clamp_latents(pre_acts, latent_first, clamp_index, clamp_value):
    columns = latent_first + jnp.arange(pre_acts.shape[1], dtype=jnp.int32)
    result = jnp.maximum(pre_acts, 0.0)
    for clamp_slot in range(clamp_index.shape[1]):
        matched = columns[None, :] == clamp_index[:, clamp_slot : clamp_slot + 1]
        result = jnp.where(matched, clamp_value[:, clamp_slot : clamp_slot + 1], result)
    return result.astype(jnp.bfloat16)


def attend(queries, key_new, value_new, cache_keys, stored_values, lengths):
    local_rows, heads_here, head_size = queries.shape
    kv_here = key_new.shape[1]
    query_group_width = heads_here // kv_here
    grouped_queries = queries.reshape(local_rows, kv_here, query_group_width, head_size)
    scaling = 1.0 / math.sqrt(head_size)
    scores = (
        jnp.einsum(
            "rkgd,rkjd->rkgj", grouped_queries, cache_keys, preferred_element_type=jnp.float32
        )
        * scaling
    )
    in_range = (
        jnp.arange(cache_keys.shape[2], dtype=jnp.int32)[None, None, None, :]
        < lengths[:, None, None, None]
    )
    scores = jnp.where(in_range, scores, -jnp.inf)
    own_score = (
        jnp.einsum("rkgd,rkd->rkg", grouped_queries, key_new, preferred_element_type=jnp.float32)
        * scaling
    )
    highest = jnp.maximum(jnp.max(scores, axis=-1), own_score)
    weights = jnp.exp(scores - highest[..., None])
    own_weight = jnp.exp(own_score - highest)
    denominator = jnp.sum(weights, axis=-1) + own_weight
    probabilities = (weights / denominator[..., None]).astype(jnp.bfloat16)
    own_prob = (own_weight / denominator).astype(jnp.bfloat16)
    blended = jnp.einsum(
        "rkgj,rkjd->rkgd", probabilities, stored_values, preferred_element_type=jnp.float32
    )
    blended = (
        blended
        + own_prob.astype(jnp.float32)[..., None] * value_new.astype(jnp.float32)[:, :, None, :]
    )
    return blended.astype(jnp.bfloat16).reshape(local_rows, heads_here * head_size)


def on_device(
    residual,
    norm_gain,
    w_query,
    key_projection_weight,
    value_projection_weight,
    w_out,
    cache_keys,
    stored_values,
    lengths,
    w_enc,
    b_enc,
    w_dec,
    b_dec,
    clamp_index,
    clamp_value,
):
    stream = residual.astype(jnp.float32)
    local_rows = residual.shape[0]
    normalized_rows = (
        stream
        * lax.rsqrt(jnp.mean(stream * stream, axis=-1, keepdims=True) + 1e-05)
        * norm_gain[None, :]
    ).astype(jnp.bfloat16)
    by_feature = lax.all_to_all(normalized_rows, "wide", split_axis=1, concat_axis=0, tiled=True)
    query_width = w_query.shape[1]
    key_width = key_projection_weight.shape[1]
    row_block = by_feature
    projected = lax.psum_scatter(
        jnp.concatenate(
            [
                jnp.dot(row_block, w_query, preferred_element_type=jnp.float32),
                jnp.dot(row_block, key_projection_weight, preferred_element_type=jnp.float32),
                jnp.dot(row_block, value_projection_weight, preferred_element_type=jnp.float32),
            ],
            axis=1,
        ),
        "wide",
        scatter_dimension=0,
        tiled=True,
    )
    heads_here = query_width // HEAD_WIDTH
    kv_here = key_width // HEAD_WIDTH
    queries = rotary(
        projected[:, :query_width].reshape(local_rows, heads_here, HEAD_WIDTH), lengths
    ).astype(jnp.bfloat16)
    key_new = rotary(
        projected[:, query_width : query_width + key_width].reshape(
            local_rows, kv_here, HEAD_WIDTH
        ),
        lengths,
    ).astype(jnp.bfloat16)
    value_new = (
        projected[:, query_width + key_width :]
        .reshape(local_rows, kv_here, HEAD_WIDTH)
        .astype(jnp.bfloat16)
    )
    attended = attend(queries, key_new, value_new, cache_keys, stored_values, lengths)
    partial_out = jnp.dot(
        lax.all_gather(attended, "wide", axis=0, tiled=True),
        w_out,
        preferred_element_type=jnp.float32,
    )
    by_row = lax.all_to_all(partial_out, "wide", split_axis=0, concat_axis=1, tiled=True)
    head_total = lax.psum_scatter(by_row, "narrow", scatter_dimension=1, tiled=True)
    width_here = w_enc.shape[0]
    narrow_index = lax.axis_index("narrow")
    own_stream = lax.dynamic_slice_in_dim(stream, narrow_index * width_here, width_here, 1)
    hidden = (own_stream + head_total).astype(jnp.bfloat16)
    partial_pre = jnp.dot(
        lax.all_gather(hidden, "wide", axis=0, tiled=True),
        w_enc,
        preferred_element_type=jnp.float32,
    )
    latents_here = w_enc.shape[1]
    latent_first = lax.axis_index("wide") * latents_here
    summed_pre = lax.psum(partial_pre, "narrow")
    activations = clamp_latents(summed_pre + b_enc[None, :], latent_first, clamp_index, clamp_value)
    row_block = activations
    rebuilt = lax.psum_scatter(
        jnp.dot(row_block, w_dec, preferred_element_type=jnp.float32),
        "wide",
        scatter_dimension=0,
        tiled=True,
    )
    return (rebuilt + b_dec[None, :]).astype(jnp.bfloat16)


def solution(mesh):
    placed = (
        P("wide", None),
        P(),
        P("wide", "narrow"),
        P("wide", "narrow"),
        P("wide", "narrow"),
        P("narrow", "wide"),
        P("wide", "narrow", None, None),
        P("wide", "narrow", None, None),
        P("wide"),
        P("narrow", "wide"),
        P("wide"),
        P("wide", "narrow"),
        P("narrow"),
        P(),
        P(),
    )
    return jax.shard_map(
        on_device, mesh=mesh, in_specs=placed, out_specs=P("wide", "narrow"), check_vma=False
    )
```

profile of v0, /device:TPU:2, one launch (start us, length us, event | category | flops | bytes accessed | tf_op | source)
XLA Modules:
  0.0 458.9 jit_solution(15226275381327403887)
XLA Ops:
  6.5 0.0 copy-start
  6.5 0.0 reduce-scatter.4.cloned.1.call-start
  6.5 1.2 multiply_reduce_fusion
  7.8 1.0 multiply_convert_fusion
  8.8 22.2 %all_to_all.38 = bf16[8,32,256]{2,0,1:T(8,128)(2,1)S(1)} all-to-all(bf16[8,32,256]{2,0,1:T(8,128)(2,1)S(1)} %bitcast.75), channel_id=1, replica_groups=mesh['wide'=32,'narrow'=8] {'wide'}, dimensions={1} | all-to-all | bytes 262144 | tf_op jit(solution)/shard_map/all_to_all | solution.py:96
  31.0 1.3 fusion.44
  32.4 0.0 copy-done.4
  32.4 0.2 fusion.40
  32.6 0.0 copy-done.5
  32.6 0.0 copy-start.9
  32.6 0.2 fusion.42
  32.8 1.2 pad_maximum_fusion
  34.0 0.0 reduce-scatter.4.cloned.1.call-update
  34.0 0.0 reduce-scatter.6.cloned.1.call-start
  34.0 0.0 copy-done.9
  34.1 0.1 iota_compare_fusion
  34.2 0.1 multiply_cosine_fusion.1
  34.3 85.1 %reduce-scatter.4.cloned.1.call-done = f32[8,1280]{1,0:T(8,128)} async-done(((f32[256,1280]{1,0:T(8,128)}), f32[8,1280]{1,0:T(8,128)}) %reduce-scatter.4.cloned.1.call-update) | async-done | bytes 40976 | tf_op jit(solution)/shard_map/reduce_scatter | solution.py:100
  119.4 0.9 slice_bitcast_fusion
  120.3 0.1 fusion.66
  120.4 0.7 slice_bitcast_fusion.1
  121.0 0.1 fusion.61
  121.2 0.1 maximum_bitcast_fusion
  121.3 0.2 fusion.56
  121.5 0.8 fusion.69
  122.2 0.2 fusion.39
  122.5 0.7 fusion.59
  123.1 0.4 fusion.16
  123.6 44.2 %all_gather.6 = bf16[256,1024]{1,0:T(8,128)(2,1)S(1)} all-gather(bf16[8,1024]{1,0:T(8,128)(2,1)S(1)} %bitcast.76), channel_id=1, replica_groups=mesh['wide'=32,'narrow'=8] {'wide'}, dimensions={0}, use_global_device_ids=true | all-gather | bytes 540672 | tf_op jit(solution)/shard_map/all_gather | solution.py:131
  167.8 0.3 convolution_bitcast_fusion
  168.1 17.8 %all_to_all.39 = f32[32,8,256]{2,1,0:T(8,128)} all-to-all(f32[32,8,256]{2,1,0:T(8,128)S(1)} %convolution_bitcast_fusion), channel_id=1, replica_groups=mesh['wide'=32,'narrow'=8] {'wide'}, dimensions={0} | all-to-all | bytes 524288 | tf_op jit(solution)/shard_map/all_to_all | solution.py:135
  185.9 0.0 reduce-scatter.6.cloned.1.call-update
  185.9 0.0 all-reduce.2.cloned.1.call-start
  186.0 33.6 %reduce-scatter.6.cloned.1.call-done = f32[8,1024]{1,0:T(8,128)} async-done(((f32[8,8192]{1,0:T(8,128)}), f32[8,1024]{1,0:T(8,128)}) %reduce-scatter.6.cloned.1.call-update) | async-done | bytes 32784 | tf_op jit(solution)/shard_map/reduce_scatter | solution.py:136
  219.6 0.8 add_convert_fusion.1
  220.4 46.2 %all_gather.7 = bf16[256,1024]{1,0:T(8,128)(2,1)S(1)} all-gather(bf16[8,1024]{1,0:T(8,128)(2,1)S(1)} %add_convert_fusion.1), channel_id=1, replica_groups=mesh['wide'=32,'narrow'=8] {'wide'}, dimensions={0}, use_global_device_ids=true | all-gather | bytes 540672 | tf_op jit(solution)/shard_map/all_gather | solution.py:142
  266.6 4.8 %fusion.70 = f32[256,2048]{1,0:T(8,128)} fusion(bf16[256,1024]{1,0:T(8,128)(2,1)S(1)} %all_gather.7, bf16[1024,2048]{1,0:T(8,128)(2,1)} %param.24), kind=kOutput, calls=%fused_computation.88 | convolution fusion | flops 1073741824 | bytes 6815744 | tf_op jit(solution)/shard_map/dot_general | solution.py:141
  271.4 0.0 all-reduce.2.cloned.1.call-update
  271.4 0.0 reduce-scatter.8.cloned.1.call-start
  271.5 0.6 copy-done.6
  272.1 0.0 copy-done.7
  272.1 82.1 %all-reduce.2.cloned.1.call-done = f32[256,2048]{1,0:T(8,128)} async-done(((f32[256,2048]{1,0:T(8,128)}), f32[256,2048]{1,0:T(8,128)}) %all-reduce.2.cloned.1.call-update) | async-done | bytes 2097168 | tf_op jit(solution)/shard_map/psum | solution.py:148
  354.3 0.0 copy-done.10
  354.3 6.1 %fusion.19 = f32[256,1024]{1,0:T(8,128)} fusion(bf16[2048,1024]{1,0:T(8,128)(2,1)} %param.26, f32[256,2048]{1,0:T(8,128)} %all-reduce.2.cloned.1.call-done, f32[2048]{0:T(1024)S(1)} %copy-done.10, f32[256]{0:T(256)S(1)} %bitcast.93, f32[256]{0:T(256)S(1)} %bitcast.94, f32[256]{0:T(256)S(1)} %bitcast.88, f32[256]{0:T(256)S(1)} %bitcast.89, ...), kind=kOutput, calls=%fused_computation.12 | convolution fusion | flops 1083179008 | bytes 7372800 | tf_op jit(solution)/shard_map/dot_general | solution.py:152
  360.4 0.0 reduce-scatter.8.cloned.1.call-update
  360.4 90.6 %reduce-scatter.8.cloned.1.call-done = f32[8,1024]{1,0:T(8,128)} async-done(((f32[256,1024]{1,0:T(8,128)}), f32[8,1024]{1,0:T(8,128)}) %reduce-scatter.8.cloned.1.call-update) | async-done | bytes 32784 | tf_op jit(solution)/shard_map/reduce_scatter | solution.py:151
  451.0 0.0 copy-done.8
  451.0 1.4 add_convert_fusion
  (24 shorter events, 0.1 us)
Async XLA Ops:
  6.5 114.9 %copy-start = (bf16[8,1,1024,128]{3,2,1,0:T(8,128)(2,1)S(1)}, bf16[8,1,1024,128]{3,2,1,0:T(8,128)(2,1)}, u32[]{:S(2)}) copy-start(bf16[8,1,1024,128]{3,2,1,0:T(8,128)(2,1)} %param.21) | copy-start | bytes 6291460
  6.5 25.8 %copy-start.4 = (bf16[256,128]{1,0:T(8,128)(2,1)S(1)}, bf16[256,128]{1,0:T(8,128)(2,1)}, u32[]{:S(2)}) copy-start(bf16[256,128]{1,0:T(8,128)(2,1)} %param.19) | copy-start | bytes 196612
  6.5 26.0 %copy-start.5 = (bf16[256,128]{1,0:T(8,128)(2,1)S(1)}, bf16[256,128]{1,0:T(8,128)(2,1)}, u32[]{:S(2)}) copy-start(bf16[256,128]{1,0:T(8,128)(2,1)} %param.18) | copy-start | bytes 196612
  6.5 112.8 %reduce-scatter.4.cloned.1.call-start = ((), (), s32[]{:S(2)}) async-start(), calls=%async_computation.5 | async-start | bytes 1351680 | tf_op jit(solution)/shard_map/reduce_scatter | solution.py:100
  32.6 1.5 copy-start.9
  34.0 185.6 %reduce-scatter.6.cloned.1.call-start = ((), (), s32[]{:S(2)}) async-start(), calls=%async_computation.6 | async-start | bytes 294912 | tf_op jit(solution)/shard_map/reduce_scatter | solution.py:136
  119.4 3.8 copy-start.1
  122.2 45.5 %copy-start.3 = (bf16[1024,256]{1,0:T(8,128)(2,1)S(1)}, bf16[1024,256]{1,0:T(8,128)(2,1)}, u32[]{:S(2)}) copy-start(bf16[1024,256]{1,0:T(8,128)(2,1)} %param.20) | copy-start | bytes 1572868
  123.1 62.8 %copy-start.2 = (bf16[8,8192]{1,0:T(8,128)(2,1)S(1)}, bf16[8,8192]{1,0:T(8,128)(2,1)}, u32[]{:S(2)}) copy-start(bf16[8,8192]{1,0:T(8,128)(2,1)} %param.15) | copy-start | bytes 393220
  185.9 168.4 %all-reduce.2.cloned.1.call-start = ((), (), s32[]{:S(2)}) async-start(), calls=%async_computation.7 | async-start | bytes 4194304 | tf_op jit(solution)/shard_map/psum | solution.py:148
  271.4 0.7 copy-start.6
  271.4 0.7 copy-start.7
  271.4 82.9 %copy-start.10 = (f32[2048]{0:T(1024)S(1)}, f32[2048]{0:T(1024)}, u32[]{:S(2)}) copy-start(f32[2048]{0:T(1024)} %param.25) | copy-start | bytes 24580
  271.4 179.6 %reduce-scatter.8.cloned.1.call-start = ((), (), s32[]{:S(2)}) async-start(), calls=%async_computation.8 | async-start | bytes 1081344 | tf_op jit(solution)/shard_map/reduce_scatter | solution.py:151
  354.3 96.7 %copy-start.8 = (f32[1024]{0:T(1024)S(1)}, f32[1024]{0:T(1024)}, u32[]{:S(2)}) copy-start(f32[1024]{0:T(1024)} %param.27) | copy-start | bytes 12292
Sparse Core Ops, SparseCore 0:
  34.1 85.2 reduce-scatter.3
  186.0 33.5 reduce-scatter.5
  271.5 82.6 all-reduce.1
  360.5 90.4 reduce-scatter.7
where the time goes:
time: 459 us
  waiting for transfers between devices  292 us (64%)
  blocking collectives  130 us (28%)
  matrix products  14.3 us (3%)
  between operations  13.3 us (3%)
  other arithmetic  6.94 us (2%)
    reduce_scatter x1, waiting for transfers between devices, on_device(): lax.psum_scatter(jnp.dot(row_block, w_dec, preferred_element_type=jnp.flo...  90.6 us
    reduce_scatter x1, waiting for transfers between devices, on_device(): lax.psum_scatter(jnp.concatenate([jnp.dot(row_block, w_query, preferred_e...  85.1 us
    psum x1, waiting for transfers between devices, on_device(): summed_pre = lax.psum(partial_pre, 'narrow')  82.1 us
    all_gather x1, blocking collectives, on_device(): lax.all_gather(hidden, 'wide', axis=0, tiled=True)  46.2 us
    all_gather x1, blocking collectives, on_device(): lax.all_gather(attended, 'wide', axis=0, tiled=True)  44.2 us
    reduce_scatter x1, waiting for transfers between devices, on_device(): lax.psum_scatter(by_row, 'narrow', scatter_dimension=1, tiled=True)  33.6 us
    all_to_all x1, blocking collectives, on_device(): lax.all_to_all(normalized_rows, 'wide', split_axis=1, concat_axis=0, tile...  22.2 us
    all_to_all x1, blocking collectives, on_device(): lax.all_to_all(partial_out, 'wide', split_axis=0, concat_axis=1, tiled=True)  17.8 us
  transfers between devices with their start and end apart: 4, of which 4 were waited for; matrix products, arithmetic and copies ran while one was open for 0% of the time, Pallas kernels for 0%

commit v1 on v0

--- a/solution.py
+++ b/solution.py
@@ -132,7 +132,9 @@
         w_out,
         preferred_element_type=jnp.float32,
     )
-    by_row = lax.all_to_all(partial_out, "wide", split_axis=0, concat_axis=1, tiled=True)
+    shards = jnp.split(partial_out, lax.axis_size("wide"), axis=0)
+    got = lax.all_to_all(jnp.stack(shards), "wide", 0, 0)
+    by_row = jnp.concatenate(got, axis=1)
     head_total = lax.psum_scatter(by_row, "narrow", scatter_dimension=1, tiled=True)
     width_here = w_enc.shape[0]
     narrow_index = lax.axis_index("narrow")

time: 459 us -> 460 us (level)
  no operation moved by 1% of the time
where the time goes in v1:
time: 460 us; the launch traced here: 459 us
  waiting for transfers between devices  292 us (63%)
  blocking collectives  131 us (28%)
  matrix products  14.3 us (3%)
  between operations  13.5 us (3%)
  other arithmetic  6.94 us (2%)
    reduce_scatter x1, waiting for transfers between devices, on_device(): lax.psum_scatter(jnp.dot(row_block, w_dec, preferred_element_type=jnp.flo...  90.6 us
    reduce_scatter x1, waiting for transfers between devices, on_device(): lax.psum_scatter(jnp.concatenate([jnp.dot(row_block, w_query, preferred_e...  85.1 us
    psum x1, waiting for transfers between devices, on_device(): summed_pre = lax.psum(partial_pre, 'narrow')  82.2 us
    all_gather x1, blocking collectives, on_device(): lax.all_gather(hidden, 'wide', axis=0, tiled=True)  46.2 us
    all_gather x1, blocking collectives, on_device(): lax.all_gather(attended, 'wide', axis=0, tiled=True)  44.3 us
    reduce_scatter x1, waiting for transfers between devices, on_device(): lax.psum_scatter(by_row, 'narrow', scatter_dimension=1, tiled=True)  33.6 us
    all_to_all x1, blocking collectives, on_device(): lax.all_to_all(normalized_rows, 'wide', split_axis=1, concat_axis=0, tile...  22.2 us
    all_to_all x1, blocking collectives, on_device(): got = lax.all_to_all(jnp.stack(shards), 'wide', 0, 0)  17.8 us
  transfers between devices with their start and end apart: 4, of which 4 were waited for; matrix products, arithmetic and copies ran while one was open for 0% of the time, Pallas kernels for 0%

profile of v1, /device:TPU:2, one launch (start us, length us, event | category | flops | bytes accessed | tf_op | source)
XLA Modules:
  0.0 459.4 jit_solution(610514241968140347)
XLA Ops:
  6.5 0.0 copy-start
  6.5 0.0 reduce-scatter.4.cloned.1.call-start
  6.5 1.2 multiply_reduce_fusion
  7.8 1.0 multiply_convert_fusion
  8.8 22.2 %all_to_all.24 = bf16[8,32,256]{2,0,1:T(8,128)(2,1)S(1)} all-to-all(bf16[8,32,256]{2,0,1:T(8,128)(2,1)S(1)} %bitcast.201), channel_id=1, replica_groups=mesh['wide'=32,'narrow'=8] {'wide'}, dimensions={1} | all-to-all | bytes 262144 | tf_op jit(solution)/shard_map/all_to_all | solution.py:96
  31.0 1.3 fusion.44
  32.4 0.0 copy-done.4
  32.4 0.2 fusion.40
  32.6 0.0 copy-done.5
  32.6 0.0 copy-start.9
  32.6 0.2 fusion.42
  32.8 1.2 pad_maximum_fusion
  34.0 0.0 reduce-scatter.4.cloned.1.call-update
  34.0 0.0 reduce-scatter.6.cloned.1.call-start
  34.0 0.0 copy-done.9
  34.1 0.1 iota_compare_fusion
  34.2 0.1 multiply_cosine_fusion.1
  34.3 85.1 %reduce-scatter.4.cloned.1.call-done = f32[8,1280]{1,0:T(8,128)} async-done(((f32[256,1280]{1,0:T(8,128)}), f32[8,1280]{1,0:T(8,128)}) %reduce-scatter.4.cloned.1.call-update) | async-done | bytes 40976 | tf_op jit(solution)/shard_map/reduce_scatter | solution.py:100
  119.4 0.9 slice_bitcast_fusion
  120.3 0.1 fusion.66
  120.4 0.7 slice_bitcast_fusion.33
  121.0 0.1 fusion.61
  121.2 0.1 maximum_bitcast_fusion
  121.3 0.2 fusion.56
  121.5 0.0 copy-done
  121.5 0.8 fusion.69
  122.2 0.2 fusion.39
  122.5 0.7 fusion.59
  123.1 0.0 copy-done.1
  123.1 0.4 fusion.16
  123.6 44.3 %all_gather.6 = bf16[256,1024]{1,0:T(8,128)(2,1)S(1)} all-gather(bf16[8,1024]{1,0:T(8,128)(2,1)S(1)} %bitcast.202), channel_id=1, replica_groups=mesh['wide'=32,'narrow'=8] {'wide'}, dimensions={0}, use_global_device_ids=true | all-gather | bytes 540672 | tf_op jit(solution)/shard_map/all_gather | solution.py:131
  167.9 0.3 fusion.70
  168.6 17.8 %all_to_all.25 = f32[32,8,256]{2,1,0:T(8,128)} all-to-all(f32[32,8,256]{2,1,0:T(8,128)S(1)} %constant_dynamic-update-slice_fusion), channel_id=1, replica_groups=mesh['wide'=32,'narrow'=8] {'wide'}, dimensions={0} | all-to-all | bytes 524288 | tf_op jit(solution)/shard_map/all_to_all | solution.py:136
  186.4 0.0 reduce-scatter.6.cloned.1.call-update
  186.4 0.0 all-reduce.2.cloned.1.call-start
  186.5 33.6 %reduce-scatter.6.cloned.1.call-done = f32[8,1024]{1,0:T(8,128)} async-done(((f32[8,8192]{1,0:T(8,128)}), f32[8,1024]{1,0:T(8,128)}) %reduce-scatter.6.cloned.1.call-update) | async-done | bytes 32784 | tf_op jit(solution)/shard_map/reduce_scatter | solution.py:138
  220.1 0.8 add_convert_fusion.1
  220.8 46.2 %all_gather.7 = bf16[256,1024]{1,0:T(8,128)(2,1)S(1)} all-gather(bf16[8,1024]{1,0:T(8,128)(2,1)S(1)} %add_convert_fusion.1), channel_id=1, replica_groups=mesh['wide'=32,'narrow'=8] {'wide'}, dimensions={0}, use_global_device_ids=true | all-gather | bytes 540672 | tf_op jit(solution)/shard_map/all_gather | solution.py:144
  267.1 4.8 %fusion.71 = f32[256,2048]{1,0:T(8,128)} fusion(bf16[256,1024]{1,0:T(8,128)(2,1)S(1)} %all_gather.7, bf16[1024,2048]{1,0:T(8,128)(2,1)} %param.24), kind=kOutput, calls=%fused_computation.152 | convolution fusion | flops 1073741824 | bytes 6815744 | tf_op jit(solution)/shard_map/dot_general | solution.py:143
  271.9 0.0 all-reduce.2.cloned.1.call-update
  271.9 0.0 reduce-scatter.8.cloned.1.call-start
  272.0 0.6 copy-done.6
  272.6 0.0 copy-done.7
  272.6 82.2 %all-reduce.2.cloned.1.call-done = f32[256,2048]{1,0:T(8,128)} async-done(((f32[256,2048]{1,0:T(8,128)}), f32[256,2048]{1,0:T(8,128)}) %all-reduce.2.cloned.1.call-update) | async-done | bytes 2097168 | tf_op jit(solution)/shard_map/psum | solution.py:150
  354.8 6.1 %fusion.19 = f32[256,1024]{1,0:T(8,128)} fusion(bf16[2048,1024]{1,0:T(8,128)(2,1)} %param.26, f32[256,2048]{1,0:T(8,128)} %all-reduce.2.cloned.1.call-done, f32[2048]{0:T(1024)S(1)} %copy-done.10, f32[256]{0:T(256)S(1)} %bitcast.219, f32[256]{0:T(256)S(1)} %bitcast.220, f32[256]{0:T(256)S(1)} %bitcast.214, f32[256]{0:T(256)S(1)} %bitcast.215, ...), kind=kOutput, calls=%fused_computation.11 | convolution fusion | flops 1083179008 | bytes 7372800 | tf_op jit(solution)/shard_map/dot_general | solution.py:154
  360.9 0.0 reduce-scatter.8.cloned.1.call-update
  361.0 90.6 %reduce-scatter.8.cloned.1.call-done = f32[8,1024]{1,0:T(8,128)} async-done(((f32[256,1024]{1,0:T(8,128)}), f32[8,1024]{1,0:T(8,128)}) %reduce-scatter.8.cloned.1.call-update) | async-done | bytes 32784 | tf_op jit(solution)/shard_map/reduce_scatter | solution.py:153
  451.5 1.4 add_convert_fusion
  (56 shorter events, 0.2 us)
Async XLA Ops:
  6.5 114.9 %copy-start = (bf16[8,1,1024,128]{3,2,1,0:T(8,128)(2,1)S(1)}, bf16[8,1,1024,128]{3,2,1,0:T(8,128)(2,1)}, u32[]{:S(2)}) copy-start(bf16[8,1,1024,128]{3,2,1,0:T(8,128)(2,1)} %param.21) | copy-start | bytes 6291460
  6.5 25.8 %copy-start.4 = (bf16[256,128]{1,0:T(8,128)(2,1)S(1)}, bf16[256,128]{1,0:T(8,128)(2,1)}, u32[]{:S(2)}) copy-start(bf16[256,128]{1,0:T(8,128)(2,1)} %param.19) | copy-start | bytes 196612
  6.5 26.0 %copy-start.5 = (bf16[256,128]{1,0:T(8,128)(2,1)S(1)}, bf16[256,128]{1,0:T(8,128)(2,1)}, u32[]{:S(2)}) copy-start(bf16[256,128]{1,0:T(8,128)(2,1)} %param.18) | copy-start | bytes 196612
  6.5 112.8 %reduce-scatter.4.cloned.1.call-start = ((), (), s32[]{:S(2)}) async-start(), calls=%async_computation.5 | async-start | bytes 1351680 | tf_op jit(solution)/shard_map/reduce_scatter | solution.py:100
  32.6 1.5 copy-start.9
  34.0 186.1 %reduce-scatter.6.cloned.1.call-start = ((), (), s32[]{:S(2)}) async-start(), calls=%async_computation.6 | async-start | bytes 294912 | tf_op jit(solution)/shard_map/reduce_scatter | solution.py:138
  119.4 3.8 copy-start.1
  122.2 45.7 %copy-start.3 = (bf16[1024,256]{1,0:T(8,128)(2,1)S(1)}, bf16[1024,256]{1,0:T(8,128)(2,1)}, u32[]{:S(2)}) copy-start(bf16[1024,256]{1,0:T(8,128)(2,1)} %param.20) | copy-start | bytes 1572868
  123.6 62.9 %copy-start.2 = (bf16[8,8192]{1,0:T(8,128)(2,1)S(1)}, bf16[8,8192]{1,0:T(8,128)(2,1)}, u32[]{:S(2)}) copy-start(bf16[8,8192]{1,0:T(8,128)(2,1)} %param.15) | copy-start | bytes 393220
  186.4 168.4 %all-reduce.2.cloned.1.call-start = ((), (), s32[]{:S(2)}) async-start(), calls=%async_computation.7 | async-start | bytes 4194304 | tf_op jit(solution)/shard_map/psum | solution.py:150
  271.9 0.7 copy-start.6
  271.9 0.7 copy-start.7
  271.9 82.9 %copy-start.10 = (f32[2048]{0:T(1024)S(1)}, f32[2048]{0:T(1024)}, u32[]{:S(2)}) copy-start(f32[2048]{0:T(1024)} %param.25) | copy-start | bytes 24580
  271.9 179.6 %reduce-scatter.8.cloned.1.call-start = ((), (), s32[]{:S(2)}) async-start(), calls=%async_computation.8 | async-start | bytes 1081344 | tf_op jit(solution)/shard_map/reduce_scatter | solution.py:153
  354.8 96.7 %copy-start.8 = (f32[1024]{0:T(1024)S(1)}, f32[1024]{0:T(1024)}, u32[]{:S(2)}) copy-start(f32[1024]{0:T(1024)} %param.27) | copy-start | bytes 12292
Sparse Core Ops, SparseCore 0:
  34.1 85.2 reduce-scatter.3
  186.5 33.5 reduce-scatter.5
  272.0 82.7 all-reduce.1
  361.1 90.4 reduce-scatter.7
